TPU v7x, 256 devices: a whole 4x4x8 slice. The times are simulated.
256 devices in a mesh: seq: 64 (over z, x, core), tensor: 4 (over y).
Axes of the slice: x: 4, y: 4, z: 8, core: 2. Of those that a mesh axis runs over, the one named last changes fastest.
Arguments:
- residual: bfloat16 [16384, 2048], P('seq', 'tensor'), may hold values from -0.29882812 to 0.29882812
- query: bfloat16 [16384, 2048], P('seq', 'tensor'), may hold values from -13 to 13
- new_keys: bfloat16 [16384, 2048], P('seq', 'tensor'), may hold values from -6 to 6
- new_values: bfloat16 [16384, 2048], P('seq', 'tensor'), may hold values from -6 to 6
- leaf_kv: bfloat16 [2, 4096, 2048], P(None, 'seq', 'tensor'), may hold values from -6 to 6
- branch_kv: bfloat16 [2, 4096, 2048], P(None, 'seq', 'tensor'), may hold values from -6 to 6
- root_kv: bfloat16 [2, 2048, 2048], P(None, 'seq', 'tensor'), may hold values from -10 to 10
- out_weight: bfloat16 [2048, 2048], P('tensor'), may hold values from -0.125 to 0.125
- norm_gain: float32 [2048], replicated, may hold values from 0.25 to 1.75
- norm_bias: float32 [2048], replicated, may hold values from -1.8 to 1.8
- up_weight: bfloat16 [2048, 4096], P(None, 'tensor'), may hold values from -0.125 to 0.125
- up_bias: float32 [4096], P('tensor'), may hold values from -3 to 3
- down_weight: bfloat16 [4096, 2048], P('tensor'), may hold values from -0.09375 to 0.09375
- down_bias: float32 [2048], replicated, may hold values from -1.8 to 1.8
- segment: int32 [64], replicated, may hold values from 0 to 15, never falling along the last dimension, each value on 1 to 8 neighbouring positions
- new_len: int32 [64], replicated, may hold values from 1 to 256, 12288 in all
Outputs:
- layer_out: bfloat16 [16384, 2048], P('seq', 'tensor')
Inputs may be any that keep to these rules, and one draw needn't show every extreme that they name: `segment`: never falling along the requests, so the requests of one branch node have consecutive indices; every node 0 to 15 has 1 to 8 requests and one has exactly 8. `new_len`: the largest is exactly 256; they sum to 12288.
All inputs are finite; a program needn't handle non-finite values.
Results may differ from a plain program's by a relative error of at most 0.018.
Values may be sent and summed in bfloat16 or wider, within the bound.
No kernel may reach another device: no remote copies, remote signals or barrier semaphores. Data moves between devices by JAX's collectives and lax.ppermute only.
A program may use at most 128 MiB of HBM per device.

v0:
```python
import jax
import jax.numpy as jnp
from jax import lax
from jax.sharding import PartitionSpec as P

HD = 128
NEGATIVE_FILL = -1e30
NORM_EPSILON = 1e-05
BLOCK_KEYS = 512


def attend(running, query_heads, key_rows, value_rows, allowed):
    largest, totals, accumulated = running
    head_count = query_heads.shape[1]
    head_width = query_heads.shape[2]
    key_heads = key_rows.reshape(key_rows.shape[0], head_count, head_width)
    value_heads = value_rows.reshape(value_rows.shape[0], head_count, head_width)
    scores = jnp.einsum(
        "qhd,khd->hqk", query_heads, key_heads, preferred_element_type=jnp.float32
    ) * head_width ** (-0.5)
    scores = jnp.where(allowed, scores, NEGATIVE_FILL)
    new_largest = jnp.maximum(largest, jnp.max(scores, axis=2))
    weights = jnp.where(allowed, jnp.exp(scores - new_largest[:, :, None]), 0.0)
    factor = jnp.exp(largest - new_largest)
    accumulated = accumulated * factor[:, :, None] + jnp.einsum(
        "hqk,khd->hqd",
        weights.astype(jnp.bfloat16),
        value_heads,
        preferred_element_type=jnp.float32,
    )
    totals = totals * factor + jnp.sum(weights, axis=2)
    return (new_largest, totals, accumulated)


def attend_blocks(running, query_heads, key_rows, value_rows):
    for block_start in range(0, key_rows.shape[0], BLOCK_KEYS):
        running = attend(
            running,
            query_heads,
            key_rows[block_start : block_start + BLOCK_KEYS],
            value_rows[block_start : block_start + BLOCK_KEYS],
            True,
        )
    return running


def per_device(
    residual,
    query,
    new_keys,
    new_values,
    leaf_kv,
    branch_kv,
    root_kv,
    out_weight,
    norm_gain,
    norm_bias,
    up_weight,
    up_bias,
    down_weight,
    down_bias,
    segment,
    new_len,
):
    row_count = query.shape[0]
    head_count = query.shape[1] // HD
    query_heads = query.reshape(row_count, head_count, HD)
    device = lax.axis_index("seq")
    my_segment = segment[device]
    branch_count = lax.axis_size("seq") // 4
    running = (
        jnp.full((head_count, row_count), NEGATIVE_FILL, jnp.float32),
        jnp.zeros((head_count, row_count), jnp.float32),
        jnp.zeros((head_count, row_count, HD), jnp.float32),
    )
    running = attend_blocks(
        running,
        query_heads,
        lax.all_gather(root_kv[0], "seq", axis=0, tiled=True),
        lax.all_gather(root_kv[1], "seq", axis=0, tiled=True),
    )
    key_rows = lax.all_gather(branch_kv[0], "seq", axis=0, tiled=True)
    value_rows = lax.all_gather(branch_kv[1], "seq", axis=0, tiled=True)
    feature_width = key_rows.shape[1]
    keys_mine = lax.dynamic_index_in_dim(
        key_rows.reshape(-1, branch_count, feature_width), my_segment, 1, keepdims=False
    )
    values_mine = lax.dynamic_index_in_dim(
        value_rows.reshape(-1, branch_count, feature_width), my_segment, 1, keepdims=False
    )
    running = attend_blocks(running, query_heads, keys_mine, values_mine)
    running = attend(running, query_heads, leaf_kv[0], leaf_kv[1], True)
    query_pos = jnp.arange(row_count, dtype=jnp.int32)
    allowed_new = (query_pos[None, :] <= query_pos[:, None]) & (
        query_pos[None, :] < new_len[device]
    )
    running = attend(running, query_heads, new_keys, new_values, allowed_new[None])
    largest, totals, accumulated = running
    attention = (
        jnp.transpose(accumulated / totals[:, :, None], (1, 0, 2))
        .reshape(row_count, head_count * HD)
        .astype(jnp.bfloat16)
    )
    projected = jnp.dot(attention, out_weight, preferred_element_type=jnp.float32)
    share_width = residual.shape[1]
    column = lax.axis_index("tensor") * share_width
    projected = lax.psum(projected.astype(jnp.bfloat16), "tensor").astype(jnp.float32)
    full_residual = lax.all_gather(residual, "tensor", axis=1, tiled=True)
    mid_full = (full_residual.astype(jnp.float32) + projected).astype(jnp.bfloat16)
    wide_mid = mid_full.astype(jnp.float32)
    row_mean = jnp.mean(wide_mid, axis=1, keepdims=True)
    row_var = jnp.mean(wide_mid * wide_mid, axis=1, keepdims=True) - row_mean * row_mean
    normed = (
        (wide_mid - row_mean) * lax.rsqrt(row_var + NORM_EPSILON) * norm_gain + norm_bias
    ).astype(jnp.bfloat16)
    up_sum = jnp.dot(normed, up_weight, preferred_element_type=jnp.float32)
    mid_share = lax.dynamic_slice_in_dim(mid_full, column, share_width, 1)
    hidden = jax.nn.gelu(up_sum + up_bias, approximate=False).astype(jnp.bfloat16)
    partial_value = jnp.dot(hidden, down_weight, preferred_element_type=jnp.float32)
    summed = lax.psum_scatter(
        partial_value.astype(jnp.bfloat16), "tensor", scatter_dimension=1, tiled=True
    ).astype(jnp.float32)
    down_share = lax.dynamic_slice_in_dim(down_bias, column, share_width, 0)
    return (summed + down_share + mid_share.astype(jnp.float32)).astype(jnp.bfloat16)


def solution(mesh):
    return jax.shard_map(
        per_device,
        mesh=mesh,
        in_specs=(
            P("seq", "tensor"),
            P("seq", "tensor"),
            P("seq", "tensor"),
            P("seq", "tensor"),
            P(None, "seq", "tensor"),
            P(None, "seq", "tensor"),
            P(None, "seq", "tensor"),
            P("tensor", None),
            P(),
            P(),
            P(None, "tensor"),
            P("tensor"),
            P("tensor", None),
            P(),
            P(),
            P(),
        ),
        out_specs=P("seq", "tensor"),
        check_vma=False,
    )
```

profile of v0, /device:TPU:2, one launch (start us, length us, event | category | flops | bytes accessed | tf_op | source)
XLA Modules:
  0.0 453.0 jit_solution(13293988858656092174)
XLA Ops:
  6.5 1.5 fusion.182
  8.2 0.7 all-gather.12.cloned.1.call-update
  8.9 1.5 fusion.181
  11.7 1.2 dynamic_slice.22
  12.9 0.6 iota_compare_fusion.1
  13.6 1.3 dynamic_slice.19
  16.2 0.9 fusion.180
  17.1 1.8 copy.117
  19.5 1.9 fusion.184
  21.4 2.0 fusion.183
  23.4 66.1 %all-gather.14.cloned.1.call-done = bf16[1,2048,512]{2,1,0:T(8,128)(2,1)} async-done(((bf16[1,32,512]{2,1,0:T(8,128)(2,1)}), bf16[1,2048,512]{2,1,0:T(8,128)(2,1)}) %all-gather.14.cloned.1.call-update) | async-done | bytes 2097168 | tf_op jit(solution)/shard_map/all_gather | solution.py:80
  89.5 2.9 fusion.178
  92.4 2.1 copy.97
  94.4 72.8 %all-gather.12.cloned.1.call-done = bf16[1,2048,512]{2,1,0:T(8,128)(2,1)} async-done(((bf16[1,32,512]{2,1,0:T(8,128)(2,1)}), bf16[1,2048,512]{2,1,0:T(8,128)(2,1)}) %all-gather.12.cloned.1.call-update) | async-done | bytes 2097168 | tf_op jit(solution)/shard_map/all_gather | solution.py:79
  167.2 2.9 fusion.179
  170.1 2.1 copy.118
  172.2 2.0 copy.120
  174.2 2.1 copy.119
  176.3 2.1 copy.121
  178.3 2.0 copy.93
  180.4 2.1 copy.89
  182.4 2.1 copy.85
  184.5 2.9 multiply_reduce_fusion
  187.4 1.7 multiply_reduce_fusion.2
  189.1 1.8 multiply_reduce_fusion.1
  190.9 2.3 multiply_reduce_fusion.3
  193.2 53.1 %all-gather.18.cloned.1.call-done = bf16[1,4096,512]{2,1,0:T(8,128)(2,1)} async-done(((bf16[1,64,512]{2,1,0:T(8,128)(2,1)}), bf16[1,4096,512]{2,1,0:T(8,128)(2,1)}) %all-gather.18.cloned.1.call-update) | async-done | bytes 4194320 | tf_op jit(solution)/shard_map/all_gather | solution.py:83
  246.3 78.8 %all-gather.16.cloned.1.call-done = bf16[1,4096,512]{2,1,0:T(8,128)(2,1)} async-done(((bf16[1,64,512]{2,1,0:T(8,128)(2,1)}), bf16[1,4096,512]{2,1,0:T(8,128)(2,1)}) %all-gather.16.cloned.1.call-update) | async-done | bytes 4194320 | tf_op jit(solution)/shard_map/all_gather | solution.py:82
  325.1 4.3 constant_dynamic-slice_fusion
  329.4 1.9 copy.122
  331.2 1.9 copy.98
  333.1 1.4 fusion.185
  334.5 0.7 fusion.176
  336.8 0.6 fusion.11
  337.9 0.6 fusion.9
  338.6 0.6 fusion.7
  340.3 0.7 fusion.23
  341.5 0.7 fusion.21
  342.5 0.7 fusion.19
  343.3 0.7 fusion.25
  344.3 1.8 convolution_convert_fusion
  346.1 5.9 %all-gather.10.cloned.1.call-done = bf16[256,2048]{1,0:T(8,128)(2,1)} async-done(((bf16[256,512]{1,0:T(8,128)(2,1)}), bf16[256,2048]{1,0:T(8,128)(2,1)}) %all-gather.10.cloned.1.call-update) | async-done | bytes 1048592 | tf_op jit(solution)/shard_map/all_gather | solution.py:108
  352.0 53.8 %all-reduce.2.cloned.1.call-done = bf16[256,2048]{1,0:T(8,128)(2,1)} async-done(((bf16[256,2048]{1,0:T(8,128)(2,1)}), bf16[256,2048]{1,0:T(8,128)(2,1)}) %all-reduce.2.cloned.1.call-update) | async-done | bytes 1048592 | tf_op jit(solution)/shard_map/psum | solution.py:107
  405.8 2.1 convert_reduce_fusion
  407.9 9.1 %convolution_convert_fusion.1 = bf16[256,2048]{1,0:T(8,128)(2,1)} fusion(bf16[1024,2048]{1,0:T(8,128)(2,1)} %param.28, bf16[2048,1024]{1,0:T(8,128)(2,1)} %param.26, bf16[256,2048]{1,0:T(8,128)(2,1)S(1)} %get-tuple-element.7, f32[2048]{0:T(1024)S(1)} %copy-done.18, f32[2048]{0:T(1024)S(1)} %copy-done.19, f32[256]{0:T(256)S(1)} %get-tuple-element.38, ...), kind=kOutput, calls=%fused_computation.4 | convolution fusion | flops 2168455168 | bytes 10508288 | tf_op jit(solution)/shard_map/dot_general | solution.py:119
  417.0 0.8 dynamic_slice.23
  417.8 26.7 %reduce-scatter.2.cloned.1.call-done = bf16[256,512]{1,0:T(8,128)(2,1)} async-done(((bf16[256,2048]{1,0:T(8,128)(2,1)}), bf16[256,512]{1,0:T(8,128)(2,1)}) %reduce-scatter.2.cloned.1.call-update) | async-done | bytes 262160 | tf_op jit(solution)/shard_map/reduce_scatter | solution.py:120
  444.4 1.7 add_convert_fusion.1
  (67 shorter events, 6.0 us)
Async XLA Ops:
  6.5 337.7 %copy-start = (bf16[512,2048]{1,0:T(8,128)(2,1)S(1)}, bf16[512,2048]{1,0:T(8,128)(2,1)}, u32[]{:S(2)}) copy-start(bf16[512,2048]{1,0:T(8,128)(2,1)} %param.23) | copy-start | bytes 6291460
  6.5 14.9 %copy-start.5 = (bf16[256,512]{1,0:T(8,128)(2,1)S(1)}, bf16[256,512]{1,0:T(8,128)(2,1)}, u32[]{:S(2)}) copy-start(bf16[256,512]{1,0:T(8,128)(2,1)} %param.17) | copy-start | bytes 786436
  6.5 82.9 %all-gather.14.cloned.1.call-start = ((), (), s32[]{:S(2)}) async-start(), calls=%async_computation.5 | async-start | bytes 2129920 | tf_op jit(solution)/shard_map/all_gather | solution.py:80
  8.1 159.1 %all-gather.12.cloned.1.call-start = ((), (), s32[]{:S(2)}) async-start(), calls=%async_computation.4 | async-start | bytes 2129920 | tf_op jit(solution)/shard_map/all_gather | solution.py:79
  8.9 237.4 %all-gather.18.cloned.1.call-start = ((), (), s32[]{:S(2)}) async-start(), calls=%async_computation.7 | async-start | bytes 4259840 | tf_op jit(solution)/shard_map/all_gather | solution.py:83
  10.5 314.7 %all-gather.16.cloned.1.call-start = ((), (), s32[]{:S(2)}) async-start(), calls=%async_computation.6 | async-start | bytes 4259840 | tf_op jit(solution)/shard_map/all_gather | solution.py:82
  11.0 340.9 %all-gather.10.cloned.1.call-start = ((), (), s32[]{:S(2)}) async-start(), calls=%async_computation.1 | async-start | bytes 1310720 | tf_op jit(solution)/shard_map/all_gather | solution.py:108
  11.6 394.2 %all-reduce.2.cloned.1.call-start = ((), (), s32[]{:S(2)}) async-start(), calls=%async_computation.2 | async-start | bytes 2097152 | tf_op jit(solution)/shard_map/psum | solution.py:107
  184.5 2.9 copy-start.12
  187.4 1.7 copy-start.11
  189.1 1.8 copy-start.10
  333.1 2.5 copy-start.15
  333.1 3.0 copy-start.14
  335.2 1.6 copy-start.1
  336.0 1.8 copy-start.2
  336.8 1.8 copy-start.3
  337.9 1.8 copy-start.4
  338.6 1.7 copy-start.16
  338.6 1.7 copy-start.17
  338.6 1.7 copy-start.9
  340.2 1.0 copy-start.13
  340.3 1.2 copy-start.8
  341.5 1.0 copy-start.7
  342.2 1.1 copy-start.6
  346.0 61.8 %copy-start.18 = (f32[2048]{0:T(1024)S(1)}, f32[2048]{0:T(1024)}, u32[]{:S(2)}) copy-start(f32[2048]{0:T(1024)} %param.25) | copy-start | bytes 24580
  346.0 61.9 %copy-start.19 = (f32[2048]{0:T(1024)S(1)}, f32[2048]{0:T(1024)}, u32[]{:S(2)}) copy-start(f32[2048]{0:T(1024)} %param.24) | copy-start | bytes 24580
  346.0 61.9 %copy-start.20 = (f32[1024]{0:T(1024)S(1)}, f32[1024]{0:T(1024)}, u32[]{:S(2)}) copy-start(f32[1024]{0:T(1024)} %param.27) | copy-start | bytes 12292
  346.1 98.4 %reduce-scatter.2.cloned.1.call-start = ((), (), s32[]{:S(2)}) async-start(), calls=%async_computation.3 | async-start | bytes 1310720 | tf_op jit(solution)/shard_map/reduce_scatter | solution.py:120
Sparse Core Ops, SparseCore 0:
  10.1 79.3 all-gather.13
  92.2 74.9 all-gather.11
  170.0 76.2 all-gather.17
  248.9 76.1 all-gather.15
  326.8 25.1 all-gather.9
  354.2 51.5 all-reduce.1
  417.1 27.2 reduce-scatter.1
where the time goes:
time: 454 us; the launch traced here: 453 us
  waiting for transfers between devices  359 us (79%)
  local copies, waits for them, and re-layouts  41.5 us (9%)
  matrix products  28.4 us (6%)
  between operations  15.7 us (3%)
  other arithmetic  8.22 us (2%)
    all_gather x1, waiting for transfers between devices, per_device(): key_rows = lax.all_gather(branch_kv[0], 'seq', axis=0, tiled=True)  78.8 us
    all_gather x1, waiting for transfers between devices, per_device(): lax.all_gather(root_kv[0], 'seq', axis=0, tiled=True)  72.8 us
    all_gather x1, waiting for transfers between devices, per_device(): lax.all_gather(root_kv[1], 'seq', axis=0, tiled=True)  66.1 us
    psum x1, waiting for transfers between devices, per_device(): lax.psum(projected.astype(jnp.bfloat16), 'tensor').astype(jnp.float32)  53.8 us
    all_gather x1, waiting for transfers between devices, per_device(): value_rows = lax.all_gather(branch_kv[1], 'seq', axis=0, tiled=True)  53.1 us
    reduce_scatter x1, waiting for transfers between devices, per_device(): lax.psum_scatter(partial_value.astype(jnp.bfloat16), 'tensor', scatter_di...  26.7 us
    dot_general x7, matrix products, attend(): jnp.einsum('qhd,khd->hqk', query_heads, key_heads, preferred_element_type...  13.9 us
    unnamed x47, local copies, waits for them, and re-layouts  12.4 us
  transfers between devices with their start and end apart: 7, of which 7 were waited for; matrix products, arithmetic and copies ran while one was open for 14% of the time, Pallas kernels for 0%

commit v1 on v0

--- a/solution.py
+++ b/solution.py
@@ -104,7 +104,9 @@
     projected = jnp.dot(attention, out_weight, preferred_element_type=jnp.float32)
     share_width = residual.shape[1]
     column = lax.axis_index("tensor") * share_width
-    projected = lax.psum(projected.astype(jnp.bfloat16), "tensor").astype(jnp.float32)
+    projected = jnp.sum(lax.all_gather(projected.astype(jnp.bfloat16), "tensor"), axis=0).astype(
+        jnp.float32
+    )
     full_residual = lax.all_gather(residual, "tensor", axis=1, tiled=True)
     mid_full = (full_residual.astype(jnp.float32) + projected).astype(jnp.bfloat16)
     wide_mid = mid_full.astype(jnp.float32)

time: 454 us -> 473 us (1.042)
  waiting for transfers between devices: 359 us -> 373 us
    psum x1 -> x0, waiting for transfers between devices: 53.8 us -> none  [per_device(): lax.psum(projected.astype(jnp.bfloat16), 'tensor').astype(jnp.float32)]
    all_gather x0 -> x1, waiting for transfers between devices: none -> 48.5 us  [per_device(): lax.all_gather(projected.astype(jnp.bfloat16), 'tensor')]
    all_gather x1, waiting for transfers between devices: 5.85 us -> 25.6 us  [per_device(): full_residual = lax.all_gather(residual, 'tensor', axis=1, tiled=True)]
  transfers between devices with their start and end apart: 7 -> 7, of which waited for: 7 -> 7; matrix products, arithmetic and copies ran while one was open for 14% -> 10% of each run, Pallas kernels for 0% -> 0%
where the time goes in v1:
time: 473 us; the launch traced here: 472 us
  waiting for transfers between devices  373 us (79%)
  local copies, waits for them, and re-layouts  41.5 us (9%)
  matrix products  28.7 us (6%)
  between operations  15.8 us (3%)
  other arithmetic  11.7 us (2%)
    all_gather x1, waiting for transfers between devices, per_device(): key_rows = lax.all_gather(branch_kv[0], 'seq', axis=0, tiled=True)  78.8 us
    all_gather x1, waiting for transfers between devices, per_device(): lax.all_gather(root_kv[0], 'seq', axis=0, tiled=True)  72.8 us
    all_gather x1, waiting for transfers between devices, per_device(): lax.all_gather(root_kv[1], 'seq', axis=0, tiled=True)  66.7 us
    all_gather x1, waiting for transfers between devices, per_device(): value_rows = lax.all_gather(branch_kv[1], 'seq', axis=0, tiled=True)  53.1 us
    all_gather x1, waiting for transfers between devices, per_device(): lax.all_gather(projected.astype(jnp.bfloat16), 'tensor')  48.5 us
    reduce_scatter x1, waiting for transfers between devices, per_device(): lax.psum_scatter(partial_value.astype(jnp.bfloat16), 'tensor', scatter_di...  26.1 us
    all_gather x1, waiting for transfers between devices, per_device(): full_residual = lax.all_gather(residual, 'tensor', axis=1, tiled=True)  25.6 us
    dot_general x7, matrix products, attend(): jnp.einsum('qhd,khd->hqk', query_heads, key_heads, preferred_element_type...  13.9 us
  transfers between devices with their start and end apart: 7, of which 7 were waited for; matrix products, arithmetic and copies ran while one was open for 10% of the time, Pallas kernels for 0%

profile of v1, /device:TPU:2, one launch (start us, length us, event | category | flops | bytes accessed | tf_op | source)
XLA Modules:
  0.0 471.6 jit_solution(3425993161807439187)
XLA Ops:
  6.5 1.5 fusion.182
  8.2 0.7 all-gather.14.cloned.1.call-update
  8.9 1.5 fusion.181
  11.1 1.2 dynamic_slice.22
  12.3 1.3 dynamic_slice.19
  15.0 0.9 fusion.180
  15.9 1.8 copy.117
  19.0 1.9 fusion.184
  20.9 2.0 fusion.183
  22.8 66.7 %all-gather.16.cloned.1.call-done = bf16[1,2048,512]{2,1,0:T(8,128)(2,1)} async-done(((bf16[1,32,512]{2,1,0:T(8,128)(2,1)}), bf16[1,2048,512]{2,1,0:T(8,128)(2,1)}) %all-gather.16.cloned.1.call-update) | async-done | bytes 2097168 | tf_op jit(solution)/shard_map/all_gather | solution.py:80
  89.5 2.9 fusion.178
  92.4 2.1 copy.97
  94.5 72.8 %all-gather.14.cloned.1.call-done = bf16[1,2048,512]{2,1,0:T(8,128)(2,1)} async-done(((bf16[1,32,512]{2,1,0:T(8,128)(2,1)}), bf16[1,2048,512]{2,1,0:T(8,128)(2,1)}) %all-gather.14.cloned.1.call-update) | async-done | bytes 2097168 | tf_op jit(solution)/shard_map/all_gather | solution.py:79
  167.2 2.9 fusion.179
  170.1 2.1 copy.118
  172.2 2.0 copy.120
  174.2 2.1 copy.119
  176.3 2.1 copy.121
  178.3 2.0 copy.93
  180.4 2.1 copy.89
  182.5 2.0 copy.85
  184.5 2.9 multiply_reduce_fusion
  187.4 1.7 multiply_reduce_fusion.2
  189.1 1.8 multiply_reduce_fusion.1
  190.9 2.3 multiply_reduce_fusion.3
  193.2 53.1 %all-gather.20.cloned.1.call-done = bf16[1,4096,512]{2,1,0:T(8,128)(2,1)} async-done(((bf16[1,64,512]{2,1,0:T(8,128)(2,1)}), bf16[1,4096,512]{2,1,0:T(8,128)(2,1)}) %all-gather.20.cloned.1.call-update) | async-done | bytes 4194320 | tf_op jit(solution)/shard_map/all_gather | solution.py:83
  246.3 78.8 %all-gather.18.cloned.1.call-done = bf16[1,4096,512]{2,1,0:T(8,128)(2,1)} async-done(((bf16[1,64,512]{2,1,0:T(8,128)(2,1)}), bf16[1,4096,512]{2,1,0:T(8,128)(2,1)}) %all-gather.18.cloned.1.call-update) | async-done | bytes 4194320 | tf_op jit(solution)/shard_map/all_gather | solution.py:82
  325.1 4.3 constant_dynamic-slice_fusion
  329.4 1.9 copy.122
  331.3 1.9 copy.98
  333.1 1.3 fusion.185
  334.5 0.7 fusion.176
  336.7 0.7 copy-done.1
  338.2 0.6 fusion.9
  339.2 0.6 fusion.7
  340.6 0.7 fusion.23
  341.5 0.7 fusion.21
  342.3 0.7 fusion.19
  343.3 0.7 fusion.25
  344.3 1.7 convolution_convert_fusion
  346.9 48.5 %all-gather.22.cloned.1.call-done = bf16[1024,2048]{1,0:T(8,128)(2,1)} async-done(((bf16[256,2048]{1,0:T(8,128)(2,1)}), bf16[1024,2048]{1,0:T(8,128)(2,1)}) %all-gather.22.cloned.1.call-update) | async-done | bytes 4194320 | tf_op jit(solution)/shard_map/all_gather | solution.py:107
  395.4 3.1 reduce_sum.121
  398.5 25.6 %all-gather.12.cloned.1.call-done = bf16[256,2048]{1,0:T(8,128)(2,1)} async-done(((bf16[256,512]{1,0:T(8,128)(2,1)}), bf16[256,2048]{1,0:T(8,128)(2,1)}) %all-gather.12.cloned.1.call-update) | async-done | bytes 1048592 | tf_op jit(solution)/shard_map/all_gather | solution.py:110
  424.1 2.5 convert_reduce_fusion
  426.6 9.5 %convolution_convert_fusion.1 = bf16[256,2048]{1,0:T(8,128)(2,1)} fusion(bf16[1024,2048]{1,0:T(8,128)(2,1)} %param.28, bf16[2048,1024]{1,0:T(8,128)(2,1)} %param.26, bf16[256,2048]{1,0:T(8,128)(2,1)} %get-tuple-element.7, f32[2048]{0:T(1024)S(1)} %copy-done.18, f32[2048]{0:T(1024)S(1)} %copy-done.19, f32[256]{0:T(256)S(1)} %get-tuple-element.38, ...), kind=kOutput, calls=%fused_computation.4 | convolution fusion | flops 2168455168 | bytes 10508288 | tf_op jit(solution)/shard_map/dot_general | solution.py:121
  436.1 0.8 dynamic_slice.23
  436.9 26.1 %reduce-scatter.2.cloned.1.call-done = bf16[256,512]{1,0:T(8,128)(2,1)} async-done(((bf16[256,2048]{1,0:T(8,128)(2,1)}), bf16[256,512]{1,0:T(8,128)(2,1)}) %reduce-scatter.2.cloned.1.call-update) | async-done | bytes 262160 | tf_op jit(solution)/shard_map/reduce_scatter | solution.py:122
  463.0 1.8 add_convert_fusion.1
  (68 shorter events, 6.6 us)
Async XLA Ops:
  6.5 337.7 %copy-start = (bf16[512,2048]{1,0:T(8,128)(2,1)S(1)}, bf16[512,2048]{1,0:T(8,128)(2,1)}, u32[]{:S(2)}) copy-start(bf16[512,2048]{1,0:T(8,128)(2,1)} %param.23) | copy-start | bytes 6291460
  6.5 14.3 %copy-start.5 = (bf16[256,512]{1,0:T(8,128)(2,1)S(1)}, bf16[256,512]{1,0:T(8,128)(2,1)}, u32[]{:S(2)}) copy-start(bf16[256,512]{1,0:T(8,128)(2,1)} %param.17) | copy-start | bytes 786436
  6.5 83.0 %all-gather.16.cloned.1.call-start = ((), (), s32[]{:S(2)}) async-start(), calls=%async_computation.4 | async-start | bytes 2129920 | tf_op jit(solution)/shard_map/all_gather | solution.py:80
  8.1 159.1 %all-gather.14.cloned.1.call-start = ((), (), s32[]{:S(2)}) async-start(), calls=%async_computation.3 | async-start | bytes 2129920 | tf_op jit(solution)/shard_map/all_gather | solution.py:79
  8.9 237.5 %all-gather.20.cloned.1.call-start = ((), (), s32[]{:S(2)}) async-start(), calls=%async_computation.6 | async-start | bytes 4259840 | tf_op jit(solution)/shard_map/all_gather | solution.py:83
  10.5 314.7 %all-gather.18.cloned.1.call-start = ((), (), s32[]{:S(2)}) async-start(), calls=%async_computation.5 | async-start | bytes 4259840 | tf_op jit(solution)/shard_map/all_gather | solution.py:82
  11.0 384.3 %all-gather.22.cloned.1.call-start = ((), (), s32[]{:S(2)}) async-start(), calls=%async_computation.7 | async-start | bytes 5242880 | tf_op jit(solution)/shard_map/all_gather | solution.py:107
  184.5 2.9 copy-start.12
  187.4 1.7 copy-start.11
  189.1 1.8 copy-start.10
  333.1 2.6 copy-start.15
  334.5 1.8 copy-start.13
  335.7 1.0 copy-start.14
  335.7 1.7 copy-start.1
  336.3 1.8 copy-start.2
  337.4 1.7 copy-start.3
  338.2 1.7 copy-start.4
  339.2 1.3 copy-start.16
  339.2 1.3 copy-start.17
  339.2 1.4 copy-start.9
  340.5 1.0 copy-start.8
  341.2 1.1 copy-start.7
  342.2 1.1 copy-start.6
  346.0 78.1 %all-gather.12.cloned.1.call-start = ((), (), s32[]{:S(2)}) async-start(), calls=%async_computation.1 | async-start | bytes 1310720 | tf_op jit(solution)/shard_map/all_gather | solution.py:110
  346.6 116.4 %reduce-scatter.2.cloned.1.call-start = ((), (), s32[]{:S(2)}) async-start(), calls=%async_computation.2 | async-start | bytes 1310720 | tf_op jit(solution)/shard_map/reduce_scatter | solution.py:122
  398.5 28.2 %copy-start.18 = (f32[2048]{0:T(1024)S(1)}, f32[2048]{0:T(1024)}, u32[]{:S(2)}) copy-start(f32[2048]{0:T(1024)} %param.25) | copy-start | bytes 24580
  398.5 28.2 %copy-start.19 = (f32[2048]{0:T(1024)S(1)}, f32[2048]{0:T(1024)}, u32[]{:S(2)}) copy-start(f32[2048]{0:T(1024)} %param.24) | copy-start | bytes 24580
  398.5 28.1 %copy-start.20 = (f32[1024]{0:T(1024)S(1)}, f32[1024]{0:T(1024)}, u32[]{:S(2)}) copy-start(f32[1024]{0:T(1024)} %param.27) | copy-start | bytes 12292
Sparse Core Ops, SparseCore 0:
  10.1 79.3 all-gather.15
  92.3 74.9 all-gather.13
  170.0 76.2 all-gather.19
  248.9 76.1 all-gather.17
  346.1 49.1 all-gather.21
  397.0 27.0 all-gather.11
  436.2 26.6 reduce-scatter.1
